TPU v7x, 512 devices: a whole 4x4x16 slice. The times are simulated.
512 devices in a mesh: seq: 64 (over y, z_hi, x, core), head: 8 (over z_lo).
Axes of the slice: x: 4, y: 4, z: 16 (z_hi: 2, z_lo: 8; z = z_hi * 8 + z_lo), core: 2. Of those that a mesh axis runs over, the one named last changes fastest.
Arguments:
- cross_q: bfloat16 [512, 2048], P('seq', 'head'), may hold values from -20 to 20
- cross_out: bfloat16 [512, 2048], P('seq', 'head'), may hold values from -0.59765625 to 0.59765625
- cross_grad: bfloat16 [512, 2048], P('seq', 'head'), may hold values from -1800 to 1800
- prefix_k: bfloat16 [8192, 2048], P('seq', 'head'), may hold values from -6 to 6
- prefix_v: bfloat16 [8192, 2048], P('seq', 'head'), may hold values from -6 to 6
- pad_counts: int32 [64], P('seq'), may hold values from 0 to 64, as said below
- self_q: bfloat16 [512, 2048], P(('seq', 'head')), may hold values from -20 to 20
- self_k: bfloat16 [512, 2048], P(('seq', 'head')), may hold values from -6 to 6
- self_v: bfloat16 [512, 2048], P(('seq', 'head')), may hold values from -6 to 6
- self_grad: bfloat16 [512, 2048], P(('seq', 'head')), may hold values from -12 to 12
Outputs:
- cross_dq: bfloat16 [512, 2048], P('seq', 'head')
- prefix_dk: bfloat16 [8192, 2048], P('seq', 'head')
- prefix_dv: bfloat16 [8192, 2048], P('seq', 'head')
- self_dq: bfloat16 [512, 2048], P('seq', 'head')
- self_dk: bfloat16 [512, 2048], P('seq', 'head')
- self_dv: bfloat16 [512, 2048], P('seq', 'head')
Inputs may be any that keep to these rules, and one draw needn't show every extreme that they name: `pad_counts`: every shard keeps at least 64 valid tokens; some shard has exactly 64 padded tokens.
All inputs are finite; a program needn't handle non-finite values.
Results may differ from a plain program's by a relative error of at most 0.0086.
Values may be sent and summed in bfloat16 or wider, within the bound.
No kernel may reach another device: no remote copies, remote signals or barrier semaphores. Data moves between devices by JAX's collectives and lax.ppermute only.
A program may use at most 64 MiB of HBM per device.

v0:
```python
import jax
import jax.numpy as jnp
from jax import lax
from jax.sharding import PartitionSpec as P

HEAD_DIM = 128


def in_one_piece(arrays, axis, dim, along):
    ends, at = ([], 0)
    for a in arrays[:-1]:
        at += a.shape[along]
        ends.append(at)
    both = jnp.concatenate(arrays, axis=along)
    return tuple(jnp.split(lax.all_gather(both, axis, axis=dim, tiled=True), ends, axis=along))


def from_everyone(x, axis):
    copies = jnp.broadcast_to(x, (lax.axis_size(axis), *x.shape))
    return lax.all_to_all(copies, axis, split_axis=0, concat_axis=0, tiled=True)


def all_in_one(x, axis):
    leaves = jax.tree.leaves(x)
    order = sorted(range(len(leaves)), key=lambda k: -leaves[k].size)
    width = (1, *leaves[order[0]].shape)[-1]
    lines = [
        jnp.pad(leaves[k].reshape(-1), (0, -leaves[k].size % width)).reshape(-1, width)
        for k in order
    ]
    both, at, found = (from_everyone(jnp.concatenate(lines), axis), 0, {})
    for k, line in zip(order, lines):
        section = both[:, at : at + len(line)].reshape(len(both), -1)
        found[k] = section[:, : leaves[k].size].reshape(-1, *leaves[k].shape)
        at += len(line)
    numbers = iter(range(len(leaves)))
    return jax.tree.map(lambda _: found[next(numbers)], x)


def joined_by_halves(pieces, combine):
    while len(jax.tree.leaves(pieces)[0]) > 1:
        pieces = jax.vmap(combine)(
            *(jax.tree.map(lambda part: part[side::2], pieces) for side in (0, 1))
        )
    return jax.tree.map(lambda part: part[0], pieces)


def merged(x, axis, combine):
    pieces = all_in_one(x, axis)
    return joined_by_halves(pieces, combine)


def split_up(x, dim, size):
    before, after = (x.shape[:dim], x.shape[dim + 1 :])
    return jnp.moveaxis(x.reshape(*before, size, -1, *after), dim, 0)


def sum_at_owner(x, axis, dim):
    size = lax.axis_size(axis)
    parts = lax.all_to_all(split_up(x, dim, size), axis, 0, 0, tiled=True)
    return jnp.sum(parts, axis=0)


def joined_along(parts, dim):
    lengths = list(parts.shape[1:])
    lengths[dim] *= parts.shape[0]
    return jnp.moveaxis(parts, 0, dim).reshape(lengths)


def gathered_copies(x, axis, dim):
    return joined_along(from_everyone(x, axis), dim)


def merge_stats(left_stats, right_stats):
    row_max = jnp.maximum(left_stats[0], right_stats[0])
    row_sum = left_stats[1] * jnp.exp(left_stats[0] - row_max) + right_stats[1] * jnp.exp(
        right_stats[0] - row_max
    )
    return (row_max, row_sum)


def head_scores(queries, key_rows, score_scale):
    return (
        jnp.einsum("qhd,khd->hqk", queries, key_rows, preferred_element_type=jnp.float32)
        * score_scale
    )


def scores_grad(weights, grad_rows, value_rows, row_dot, score_scale):
    grad_probs = jnp.einsum(
        "qhd,khd->hqk", grad_rows, value_rows, preferred_element_type=jnp.float32
    )
    return (weights * (grad_probs - jnp.transpose(row_dot)[:, :, None]) * score_scale).astype(
        jnp.bfloat16
    )


def contract_rows(left_rows, right_rows):
    return jnp.einsum("hqk,qhd->khd", left_rows, right_rows, preferred_element_type=jnp.float32)


def contract_cols(left_rows, right_rows):
    return jnp.einsum("hqk,khd->qhd", left_rows, right_rows, preferred_element_type=jnp.float32)


SEQ_PARTS = ("c", "x", "zh", "y")


def gather_seq(x, dim):
    for axis in SEQ_PARTS:
        x = lax.all_gather(x, axis, axis=dim, tiled=True)
    return x


def merged_seq(row_max, row_sum):
    for axis in SEQ_PARTS:
        both = lax.all_gather(jnp.stack([row_max, row_sum]), axis)
        top = jnp.max(both[:, 0], axis=0)
        row_sum = jnp.sum(both[:, 1] * jnp.exp(both[:, 0] - top), axis=0)
        row_max = top
    return (row_max, row_sum)


def shards(
    cross_q,
    cross_out,
    cross_grad,
    prefix_k,
    prefix_v,
    pad_counts,
    self_q,
    self_k,
    self_v,
    self_grad,
):
    score_scale = HEAD_DIM ** (-0.5)
    own_rows, feature_width = cross_q.shape
    local_heads = feature_width // HEAD_DIM
    tokens = prefix_k.shape[0]
    grad_own = cross_grad.reshape(own_rows, local_heads, HEAD_DIM).astype(jnp.float32)
    out_own = cross_out.reshape(own_rows, local_heads, HEAD_DIM).astype(jnp.float32)
    row_dot = jnp.sum(grad_own * out_own, axis=2).astype(jnp.bfloat16)
    stacked = jnp.stack([self_q, self_k, self_v, self_grad])
    regrouped = lax.all_to_all(stacked, "zl", split_axis=2, concat_axis=1, tiled=True)
    block_rows = regrouped.shape[1]
    self_cols = jnp.transpose(regrouped, (1, 0, 2)).reshape(block_rows, -1)
    pieces = (cross_q, cross_grad, row_dot, self_cols)
    ends, at = ([], 0)
    for piece in pieces[:-1]:
        at += piece.shape[1]
        ends.append(at)
    gathered = gather_seq(jnp.concatenate(pieces, axis=1), 0)
    query_all, grad_all, dots_all, self_all = jnp.split(gathered, ends, axis=1)
    latents = query_all.shape[0]
    query_heads = query_all.reshape(latents, local_heads, HEAD_DIM)
    grad_heads = grad_all.reshape(latents, local_heads, HEAD_DIM)
    key_heads = prefix_k.reshape(tokens, local_heads, HEAD_DIM)
    value_heads = prefix_v.reshape(tokens, local_heads, HEAD_DIM)
    valid_keys = jnp.arange(tokens) < tokens - pad_counts[0]
    scores = head_scores(query_heads, key_heads, score_scale)
    scores = jnp.where(valid_keys[None, None, :], scores, -jnp.inf)
    row_max = jnp.max(scores, axis=2)
    row_sum = jnp.sum(jnp.exp(scores - row_max[:, :, None]), axis=2)
    row_maxes, row_sums = merged_seq(row_max, row_sum)
    log_total = row_maxes + jnp.log(row_sums)
    row_dots = dots_all.astype(jnp.float32)
    weights = jnp.exp(scores - log_total[:, :, None])
    prefix_dv = (
        contract_rows(weights.astype(jnp.bfloat16), grad_heads)
        .reshape(tokens, feature_width)
        .astype(jnp.bfloat16)
    )
    grad_scores = scores_grad(weights, grad_heads, value_heads, row_dots, score_scale)
    prefix_dk = (
        contract_rows(grad_scores, query_heads).reshape(tokens, feature_width).astype(jnp.bfloat16)
    )
    partial_value = contract_cols(grad_scores, key_heads).reshape(latents, feature_width)
    cross_dq = sum_at_owner(partial_value, SEQ_AXES, 0).astype(jnp.bfloat16)
    everything = jnp.transpose(self_all.reshape(latents, 4, feature_width), (1, 0, 2))
    row_start = lax.axis_index(SEQ_AXES) * block_rows
    all_rows = everything.shape[1]
    query_every = everything[0].reshape(all_rows, local_heads, HEAD_DIM)
    key_every = everything[1].reshape(all_rows, local_heads, HEAD_DIM)
    value_every = everything[2].reshape(all_rows, local_heads, HEAD_DIM)
    grad_every = everything[3].reshape(all_rows, local_heads, HEAD_DIM)
    row_ids = jnp.arange(all_rows)
    causal_full = row_ids[:, None] >= row_ids[None, :]
    full_scores = head_scores(query_every, key_every, score_scale)
    full_scores = jnp.where(causal_full[None, :, :], full_scores, -jnp.inf)
    full_lse = jax.nn.logsumexp(full_scores, axis=2)
    full_weights = jnp.exp(full_scores - full_lse[:, :, None])
    full_half = full_weights.astype(jnp.bfloat16)
    full_out = contract_cols(full_half, value_every)
    full_dot = jnp.sum(grad_every.astype(jnp.float32) * full_out, axis=2)
    full_gs = scores_grad(full_weights, grad_every, value_every, full_dot, score_scale)
    query_part = lax.dynamic_slice_in_dim(full_gs, row_start, block_rows, 1)
    self_dq = (
        contract_cols(query_part, key_every).reshape(block_rows, feature_width).astype(jnp.bfloat16)
    )
    key_part = lax.dynamic_slice_in_dim(full_gs, row_start, block_rows, 2)
    half_part = lax.dynamic_slice_in_dim(full_half, row_start, block_rows, 2)
    self_dk = (
        contract_rows(key_part, query_every).reshape(block_rows, feature_width).astype(jnp.bfloat16)
    )
    self_dv = (
        contract_rows(half_part, grad_every).reshape(block_rows, feature_width).astype(jnp.bfloat16)
    )
    return (cross_dq, prefix_dk, prefix_dv, self_dq, self_dk, self_dv)


SEQ_AXES = ("y", "zh", "x", "c")


def solution(mesh):
    sizes = dict(mesh.shape)
    split = mesh.devices.reshape(4, 2, 4, 2, sizes["head"])
    mesh = jax.sharding.Mesh(split, (*SEQ_AXES, "zl"))
    in_specs = (
        P(SEQ_AXES, "zl"),
        P(SEQ_AXES, "zl"),
        P(SEQ_AXES, "zl"),
        P(SEQ_AXES, "zl"),
        P(SEQ_AXES, "zl"),
        P(SEQ_AXES),
        P((*SEQ_AXES, "zl"), None),
        P((*SEQ_AXES, "zl"), None),
        P((*SEQ_AXES, "zl"), None),
        P((*SEQ_AXES, "zl"), None),
    )
    out_specs = (
        P(SEQ_AXES, "zl"),
        P(SEQ_AXES, "zl"),
        P(SEQ_AXES, "zl"),
        P(SEQ_AXES, "zl"),
        P(SEQ_AXES, "zl"),
        P(SEQ_AXES, "zl"),
    )
    return jax.shard_map(shards, mesh=mesh, in_specs=in_specs, out_specs=out_specs, check_vma=False)
```

profile of v0, /device:TPU:33, one launch (start us, length us, event | category | flops | bytes accessed | tf_op | source)
XLA Modules:
  0.0 228.5 jit_solution(2826771414848816739)
XLA Ops:
  7.2 0.0 copy-start
  7.2 0.0 copy-start.3
  7.2 0.0 copy-start.4
  7.2 0.8 pad_maximum_fusion
  8.0 0.9 copy.128
  9.0 0.5 broadcast.35
  9.5 0.0 copy-start.5
  9.5 11.6 %reduce.4 = bf16[2048,4]{1,0:T(8,128)(2,1)S(1)} reduce(bf16[2048,1,4]{2,1,0:T(2,128)(2,1)S(1)} %bitcast.168, bf16[]{:T(256)} %broadcast.35), dimensions={1}, to_apply=%bitcast.135.reduce_sub_computation | reduce | bytes 32770
  21.1 1.4 reshape.100
  22.5 12.1 %all-to-all-start = ((bf16[8,2,512]{2,1,0:T(2,128)(2,1)}), bf16[8,2,512]{2,1,0:T(2,128)(2,1)S(1)}, u32[]{:S(2)}, u32[]{:S(2)}) async-start(bf16[8,2,512]{2,1,0:T(2,128)(2,1)} %reshape.100), calls=%async_computation | async-start | bytes 32768 | tf_op jit(solution)/shard_map/all_to_all | solution.py:144
  34.5 0.0 all-gather.6.cloned.1.call-start
  34.5 0.0 copy-done.3
  34.5 0.0 copy-done.4
  34.6 0.1 bitcast_reduce_fusion.4
  34.6 0.1 copy.130
  34.7 7.9 %all-to-all-done = bf16[8,2,512]{2,1,0:T(2,128)(2,1)S(1)} async-done(((bf16[8,2,512]{2,1,0:T(2,128)(2,1)}), bf16[8,2,512]{2,1,0:T(2,128)(2,1)S(1)}, u32[]{:S(2)}, u32[]{:S(2)}) %all-to-all-start) | async-done | bytes 16416 | tf_op jit(solution)/shard_map/all_to_all | solution.py:144
  42.7 1.4 reshape.101
  44.1 0.6 copy.129
  44.6 0.0 copy-done.5
  44.7 0.1 concatenate.3
  44.8 3.6 %all_gather.36 = bf16[16,1538]{1,0:T(8,128)(2,1)S(1)} all-gather(bf16[8,1538]{1,0:T(8,128)(2,1)S(1)} %concatenate.3), channel_id=1, replica_groups=mesh['y'=4,'zh'=2,'x'=4,'c'=2,'zl'=8] {'c'}, dimensions={0}, use_global_device_ids=true | all-gather | bytes 73824 | tf_op jit(solution)/shard_map/all_gather | solution.py:111
  48.4 10.1 %all_gather.37 = bf16[64,1538]{1,0:T(8,128)(2,1)S(1)} all-gather(bf16[16,1538]{1,0:T(8,128)(2,1)S(1)} %all_gather.36), channel_id=1, replica_groups=mesh['y'=4,'zh'=2,'x'=4,'c'=2,'zl'=8] {'x'}, dimensions={0}, use_global_device_ids=true | all-gather | bytes 246080 | tf_op jit(solution)/shard_map/all_gather | solution.py:111
  58.4 30.3 %all_gather.38 = bf16[128,1538]{1,0:T(8,128)(2,1)} all-gather(bf16[64,1538]{1,0:T(8,128)(2,1)S(1)} %all_gather.37), channel_id=1, replica_groups=mesh['y'=4,'zh'=2,'x'=4,'c'=2,'zl'=8] {'zh'}, dimensions={0}, use_global_device_ids=true | all-gather | bytes 590592 | tf_op jit(solution)/shard_map/all_gather | solution.py:111
  88.8 0.0 all-gather.6.cloned.1.call-update
  89.5 0.1 iota_compare_fusion
  89.5 30.5 %all-gather.6.cloned.1.call-done = bf16[512,1538]{1,0:T(8,128)(2,1)} async-done(((bf16[128,1538]{1,0:T(8,128)(2,1)}), bf16[512,1538]{1,0:T(8,128)(2,1)}) %all-gather.6.cloned.1.call-update) | async-done | bytes 1574928 | tf_op jit(solution)/shard_map/all_gather | solution.py:111
  120.0 0.9 convert_bitcast_fusion
  121.0 0.1 copy.141
  121.1 1.1 fusion.37
  122.2 0.0 copy-start.2
  122.2 0.1 copy.131
  122.3 0.1 copy.138
  122.5 0.0 copy-done
  122.5 0.2 fusion.39
  122.7 0.0 copy-start.1
  122.7 0.1 exponential_reduce_fusion.1
  122.8 2.3 %all-gather = f32[4,2,512]{2,1,0:T(2,128)S(1)} all-gather(f32[2,2,512]{2,1,0:T(2,128)S(1)} %pad_maximum_fusion.1), channel_id=2, replica_groups=mesh['y'=4,'zh'=2,'x'=4,'c'=2,'zl'=8] {'c'}, dimensions={0}, use_global_device_ids=true | all-gather | bytes 24576 | tf_op jit(solution)/shard_map/all_gather | solution.py:117
  125.2 9.3 %all-gather.1 = f32[8,2,512]{2,1,0:T(2,128)S(1)} all-gather(f32[2,2,512]{2,1,0:T(2,128)S(1)} %pad_maximum_fusion.2), channel_id=3, replica_groups=mesh['y'=4,'zh'=2,'x'=4,'c'=2,'zl'=8] {'x'}, dimensions={0}, use_global_device_ids=true | all-gather | bytes 40960 | tf_op jit(solution)/shard_map/all_gather | solution.py:117
  134.6 11.9 %all-gather.2 = f32[4,2,512]{2,1,0:T(2,128)S(1)} all-gather(f32[2,2,512]{2,1,0:T(2,128)S(1)} %pad_maximum_fusion.3), channel_id=4, replica_groups=mesh['y'=4,'zh'=2,'x'=4,'c'=2,'zl'=8] {'zh'}, dimensions={0}, use_global_device_ids=true | all-gather | bytes 24576 | tf_op jit(solution)/shard_map/all_gather | solution.py:117
  146.6 9.0 %all-gather.3 = f32[8,2,512]{2,1,0:T(2,128)S(1)} all-gather(f32[2,2,512]{2,1,0:T(2,128)S(1)} %pad_maximum_fusion.4), channel_id=5, replica_groups=mesh['y'=4,'zh'=2,'x'=4,'c'=2,'zl'=8] {'y'}, dimensions={0}, use_global_device_ids=true | all-gather | bytes 40960 | tf_op jit(solution)/shard_map/all_gather | solution.py:117
  155.7 0.3 convolution_convert_fusion
  155.9 0.0 copy-done.2
  155.9 0.2 fusion.5
  156.1 0.2 convolution_convert_fusion.1
  156.4 0.3 convolution_bitcast_fusion.1
  156.7 0.0 copy-done.1
  156.7 0.6 split.19
  157.3 0.5 copy.177
  157.9 0.1 fusion.38
  157.9 0.7 copy.159
  158.7 0.7 copy.160
  159.4 0.4 copy.145
  159.8 1.2 reshape_reshape.3
  161.0 21.8 %all-to-all-start.1 = ((f32[64,8,256]{2,1,0:T(8,128)}), f32[64,8,256]{2,1,0:T(8,128)S(1)}, u32[]{:S(2)}, u32[]{:S(2)}) async-start(f32[64,8,256]{2,1,0:T(8,128)} %reshape_reshape.3), calls=%async_computation.1 | async-start | bytes 1048576 | tf_op jit(solution)/shard_map/all_to_all | solution.py:60
  182.9 0.6 fusion.40
  183.5 0.3 exponential_reduce_fusion
  183.8 0.3 fusion
  184.1 0.8 fusion.8
  184.9 0.3 fusion.6
  185.2 0.6 multiply_convert_fusion
  185.9 0.8 fusion.7
  186.6 1.0 fusion.9
  187.6 33.4 %all-to-all-done.1 = f32[64,8,256]{2,1,0:T(8,128)S(1)} async-done(((f32[64,8,256]{2,1,0:T(8,128)}), f32[64,8,256]{2,1,0:T(8,128)S(1)}, u32[]{:S(2)}, u32[]{:S(2)}) %all-to-all-start.1) | async-done | bytes 524320 | tf_op jit(solution)/shard_map/all_to_all | solution.py:60
  221.0 0.7 reduce_sum.87
  (17 shorter events, 0.2 us)
Async XLA Ops:
  7.2 115.3 %copy-start = (bf16[128,256]{1,0:T(8,128)(2,1)S(1)}, bf16[128,256]{1,0:T(8,128)(2,1)}, u32[]{:S(2)}) copy-start(bf16[128,256]{1,0:T(8,128)(2,1)} %param.13) | copy-start | bytes 196612
  7.2 27.4 %copy-start.3 = (bf16[8,256]{1,0:T(8,128)(2,1)S(1)}, bf16[8,256]{1,0:T(8,128)(2,1)}, u32[]{:S(2)}) copy-start(bf16[8,256]{1,0:T(8,128)(2,1)} %param.12) | copy-start | bytes 12292
  7.2 27.4 %copy-start.4 = (bf16[8,256]{1,0:T(8,128)(2,1)S(1)}, bf16[8,256]{1,0:T(8,128)(2,1)}, u32[]{:S(2)}) copy-start(bf16[8,256]{1,0:T(8,128)(2,1)} %param.11) | copy-start | bytes 12292
  9.5 35.2 %copy-start.5 = (bf16[8,256]{1,0:T(8,128)(2,1)S(1)}, bf16[8,256]{1,0:T(8,128)(2,1)}, u32[]{:S(2)}) copy-start(bf16[8,256]{1,0:T(8,128)(2,1)} %param.10) | copy-start | bytes 12292
  22.5 20.2 %all-to-all-start = ((bf16[8,2,512]{2,1,0:T(2,128)(2,1)}), bf16[8,2,512]{2,1,0:T(2,128)(2,1)S(1)}, u32[]{:S(2)}, u32[]{:S(2)}) async-start(bf16[8,2,512]{2,1,0:T(2,128)(2,1)} %reshape.100), calls=%async_computation | async-start | bytes 32768 | tf_op jit(solution)/shard_map/all_to_all | solution.py:144
  34.5 85.5 %all-gather.6.cloned.1.call-start = ((), (), s32[]{:S(2)}) async-start(), calls=%async_computation.2 | async-start | bytes 2129920 | tf_op jit(solution)/shard_map/all_gather | solution.py:111
  122.2 33.8 %copy-start.2 = (bf16[128,256]{1,0:T(8,128)(2,1)S(1)}, bf16[128,256]{1,0:T(8,128)(2,1)}, u32[]{:S(2)}) copy-start(bf16[128,256]{1,0:T(8,128)(2,1)} %param.14) | copy-start | bytes 196612
  122.7 34.0 %copy-start.1 = (bf16[512,1538]{1,0:T(8,128)(2,1)S(1)}, bf16[512,1538]{1,0:T(8,128)(2,1)}, u32[]{:S(2)}) copy-start(bf16[512,1538]{1,0:T(8,128)(2,1)} %all-gather.6.cloned.1.call-done) | copy-start | bytes 4724740
  161.0 59.9 %all-to-all-start.1 = ((f32[64,8,256]{2,1,0:T(8,128)}), f32[64,8,256]{2,1,0:T(8,128)S(1)}, u32[]{:S(2)}, u32[]{:S(2)}) async-start(f32[64,8,256]{2,1,0:T(8,128)} %reshape_reshape.3), calls=%async_computation.1 | async-start | bytes 1048576 | tf_op jit(solution)/shard_map/all_to_all | solution.py:60
Sparse Core Ops, SparseCore 0:
  88.9 31.0 all-gather.5
where the time goes:
time: 229 us; the launch traced here: 228 us
  blocking collectives  76.6 us (33%)
  waiting for transfers between devices  71.8 us (31%)
  starting transfers between devices  33.9 us (15%)
  other arithmetic  15.1 us (7%)
  between operations  15 us (7%)
  local copies, waits for them, and re-layouts  10.9 us (5%)
  matrix products  5.29 us (2%)
    all_gather x3, blocking collectives, gather_seq(): x = lax.all_gather(x, axis, axis=dim, tiled=True)  44 us
    all_to_all x1, waiting for transfers between devices, sum_at_owner(): parts = lax.all_to_all(split_up(x, dim, size), axis, 0, 0, tiled=True)  33.4 us
    all_gather x4, blocking collectives, merged_seq(): both = lax.all_gather(jnp.stack([row_max, row_sum]), axis)  32.6 us
    all_gather x1, waiting for transfers between devices, gather_seq(): x = lax.all_gather(x, axis, axis=dim, tiled=True)  30.5 us
    all_to_all x1, starting transfers between devices, sum_at_owner(): parts = lax.all_to_all(split_up(x, dim, size), axis, 0, 0, tiled=True)  21.8 us
    all_to_all x1, starting transfers between devices, shards(): lax.all_to_all(stacked, 'zl', split_axis=2, concat_axis=1, tiled=True)  12.1 us
    unnamed x1, other arithmetic  11.6 us
    all_to_all x1, waiting for transfers between devices, shards(): lax.all_to_all(stacked, 'zl', split_axis=2, concat_axis=1, tiled=True)  7.93 us
  transfers between devices with their start and end apart: 3, of which 3 were waited for; matrix products, arithmetic and copies ran while one was open for 2% of the time, Pallas kernels for 0%

commit v1 on v0

--- a/solution.py
+++ b/solution.py
@@ -141,7 +141,9 @@
     out_own = cross_out.reshape(own_rows, local_heads, HEAD_DIM).astype(jnp.float32)
     row_dot = jnp.sum(grad_own * out_own, axis=2).astype(jnp.bfloat16)
     stacked = jnp.stack([self_q, self_k, self_v, self_grad])
-    regrouped = lax.all_to_all(stacked, "zl", split_axis=2, concat_axis=1, tiled=True)
+    regrouped = jnp.concatenate(
+        jax.lax.all_to_all(jnp.stack(jnp.split(stacked, jax.lax.axis_size("zl"), 2)), "zl", 0, 0), 1
+    )
     block_rows = regrouped.shape[1]
     self_cols = jnp.transpose(regrouped, (1, 0, 2)).reshape(block_rows, -1)
     pieces = (cross_q, cross_grad, row_dot, self_cols)

time: 229 us -> 220 us (0.961)
  other arithmetic: 15.1 us -> 3.3 us
    unnamed x1 -> x0, other arithmetic: 11.6 us -> none
    unnamed x18 -> x16, local copies, waits for them, and re-layouts: 4.82 us -> 5.57 us
  transfers between devices with their start and end apart: 3 -> 3, of which waited for: 3 -> 3; matrix products, arithmetic and copies ran while one was open for 2% -> 3% of each run, Pallas kernels for 0% -> 0%
where the time goes in v1:
time: 220 us; the launch traced here: 219 us
  blocking collectives  77.7 us (35%)
  waiting for transfers between devices  72.8 us (33%)
  starting transfers between devices  34 us (15%)
  between operations  14.9 us (7%)
  local copies, waits for them, and re-layouts  11.1 us (5%)
  matrix products  5.28 us (2%)
  other arithmetic  3.3 us (2%)
    all_gather x3, blocking collectives, gather_seq(): x = lax.all_gather(x, axis, axis=dim, tiled=True)  43.9 us
    all_gather x4, blocking collectives, merged_seq(): both = lax.all_gather(jnp.stack([row_max, row_sum]), axis)  33.8 us
    all_to_all x1, waiting for transfers between devices, sum_at_owner(): parts = lax.all_to_all(split_up(x, dim, size), axis, 0, 0, tiled=True)  33.4 us
    all_gather x1, waiting for transfers between devices, gather_seq(): x = lax.all_gather(x, axis, axis=dim, tiled=True)  32.2 us
    all_to_all x1, starting transfers between devices, sum_at_owner(): parts = lax.all_to_all(split_up(x, dim, size), axis, 0, 0, tiled=True)  21.9 us
    all_to_all x1, starting transfers between devices, shards(): jax.lax.all_to_all(jnp.stack(jnp.split(stacked, jax.lax.axis_size('zl'),...  12.1 us
    all_to_all x1, waiting for transfers between devices, shards(): jax.lax.all_to_all(jnp.stack(jnp.split(stacked, jax.lax.axis_size('zl'),...  7.24 us
    unnamed x16, local copies, waits for them, and re-layouts  5.57 us
  transfers between devices with their start and end apart: 3, of which 3 were waited for; matrix products, arithmetic and copies ran while one was open for 3% of the time, Pallas kernels for 0%

profile of v1, /device:TPU:33, one launch (start us, length us, event | category | flops | bytes accessed | tf_op | source)
XLA Modules:
  0.0 219.1 jit_solution(18412205469411828668)
XLA Ops:
  7.2 0.0 copy-start
  7.2 0.8 pad_maximum_fusion
  8.0 0.6 constant_dynamic-update-slice_fusion.7
  8.6 0.6 constant_dynamic-update-slice_fusion.6
  9.2 0.6 constant_dynamic-update-slice_fusion.5
  9.8 0.6 constant_dynamic-update-slice_fusion.4
  10.3 0.6 constant_dynamic-update-slice_fusion.3
  10.9 0.6 constant_dynamic-update-slice_fusion.2
  11.5 0.6 constant_dynamic-update-slice_fusion.1
  12.1 0.6 constant_dynamic-update-slice_fusion
  12.7 12.1 %all-to-all-start = ((bf16[8,4,1,256]{3,1,2,0:T(4,128)(2,1)}), bf16[8,4,1,256]{3,1,2,0:T(4,128)(2,1)S(1)}, u32[]{:S(2)}, u32[]{:S(2)}) async-start(bf16[8,4,1,256]{3,1,2,0:T(4,128)(2,1)} %constant_dynamic-update-slice_fusion), calls=%async_computation | async-start | bytes 32768 | tf_op jit(solution)/shard_map/all_to_all | solution.py:145
  24.7 0.0 all-gather.6.cloned.1.call-start
  24.7 0.8 bitcast_reduce_fusion.4
  25.5 0.1 copy.101
  25.6 7.2 %all-to-all-done = bf16[8,4,1,256]{3,1,2,0:T(4,128)(2,1)S(1)} async-done(((bf16[8,4,1,256]{3,1,2,0:T(4,128)(2,1)}), bf16[8,4,1,256]{3,1,2,0:T(4,128)(2,1)S(1)}, u32[]{:S(2)}, u32[]{:S(2)}) %all-to-all-start) | async-done | bytes 16416 | tf_op jit(solution)/shard_map/all_to_all | solution.py:145
  32.9 0.8 concatenate.3
  33.7 3.6 %all_gather.36 = bf16[16,1538]{1,0:T(8,128)(2,1)S(1)} all-gather(bf16[8,1538]{1,0:T(8,128)(2,1)S(1)} %concatenate.3), channel_id=1, replica_groups=mesh['y'=4,'zh'=2,'x'=4,'c'=2,'zl'=8] {'c'}, dimensions={0}, use_global_device_ids=true | all-gather | bytes 73824 | tf_op jit(solution)/shard_map/all_gather | solution.py:111
  37.3 10.1 %all_gather.37 = bf16[64,1538]{1,0:T(8,128)(2,1)S(1)} all-gather(bf16[16,1538]{1,0:T(8,128)(2,1)S(1)} %all_gather.36), channel_id=1, replica_groups=mesh['y'=4,'zh'=2,'x'=4,'c'=2,'zl'=8] {'x'}, dimensions={0}, use_global_device_ids=true | all-gather | bytes 246080 | tf_op jit(solution)/shard_map/all_gather | solution.py:111
  47.3 30.2 %all_gather.38 = bf16[128,1538]{1,0:T(8,128)(2,1)S(1)} all-gather(bf16[64,1538]{1,0:T(8,128)(2,1)S(1)} %all_gather.37), channel_id=1, replica_groups=mesh['y'=4,'zh'=2,'x'=4,'c'=2,'zl'=8] {'zh'}, dimensions={0}, use_global_device_ids=true | all-gather | bytes 590592 | tf_op jit(solution)/shard_map/all_gather | solution.py:111
  77.6 0.9 copy.102
  78.5 0.0 all-gather.6.cloned.1.call-update
  78.5 0.0 copy-start.2
  79.2 0.1 iota_compare_fusion
  79.3 32.2 %all-gather.6.cloned.1.call-done = bf16[512,1538]{0,1:T(8,128)(2,1)} async-done(((bf16[128,1538]{0,1:T(8,128)(2,1)}), bf16[512,1538]{0,1:T(8,128)(2,1)}) %all-gather.6.cloned.1.call-update) | async-done | bytes 1574928 | tf_op jit(solution)/shard_map/all_gather | solution.py:111
  111.5 0.0 copy-start.1
  111.5 1.2 fusion.37
  112.7 0.0 copy-done
  112.7 0.2 fusion.39
  113.0 0.1 exponential_reduce_fusion.1
  113.1 3.0 %all-gather = f32[4,2,512]{2,1,0:T(2,128)S(1)} all-gather(f32[2,2,512]{2,1,0:T(2,128)S(1)} %pad_maximum_fusion.1), channel_id=2, replica_groups=mesh['y'=4,'zh'=2,'x'=4,'c'=2,'zl'=8] {'c'}, dimensions={0}, use_global_device_ids=true | all-gather | bytes 24576 | tf_op jit(solution)/shard_map/all_gather | solution.py:117
  116.2 9.6 %all-gather.1 = f32[8,2,512]{2,1,0:T(2,128)S(1)} all-gather(f32[2,2,512]{2,1,0:T(2,128)S(1)} %pad_maximum_fusion.2), channel_id=3, replica_groups=mesh['y'=4,'zh'=2,'x'=4,'c'=2,'zl'=8] {'x'}, dimensions={0}, use_global_device_ids=true | all-gather | bytes 40960 | tf_op jit(solution)/shard_map/all_gather | solution.py:117
  125.8 11.9 %all-gather.2 = f32[4,2,512]{2,1,0:T(2,128)S(1)} all-gather(f32[2,2,512]{2,1,0:T(2,128)S(1)} %pad_maximum_fusion.3), channel_id=4, replica_groups=mesh['y'=4,'zh'=2,'x'=4,'c'=2,'zl'=8] {'zh'}, dimensions={0}, use_global_device_ids=true | all-gather | bytes 24576 | tf_op jit(solution)/shard_map/all_gather | solution.py:117
  137.8 9.2 %all-gather.3 = f32[8,2,512]{2,1,0:T(2,128)S(1)} all-gather(f32[2,2,512]{2,1,0:T(2,128)S(1)} %pad_maximum_fusion.4), channel_id=5, replica_groups=mesh['y'=4,'zh'=2,'x'=4,'c'=2,'zl'=8] {'y'}, dimensions={0}, use_global_device_ids=true | all-gather | bytes 40960 | tf_op jit(solution)/shard_map/all_gather | solution.py:117
  147.1 0.2 convolution_convert_fusion
  147.3 0.0 copy-done.1
  147.4 0.0 copy-done.2
  147.4 0.2 fusion.5
  147.6 0.2 convolution_convert_fusion.1
  147.8 0.3 convolution_bitcast_fusion.1
  148.1 0.2 split.59
  148.4 0.1 fusion.38
  148.4 0.7 copy.127
  149.2 0.7 copy.128
  149.9 0.4 copy.114
  150.3 1.2 reshape_reshape.3
  151.5 21.9 %all-to-all-start.1 = ((f32[64,8,256]{2,1,0:T(8,128)}), f32[64,8,256]{2,1,0:T(8,128)S(1)}, u32[]{:S(2)}, u32[]{:S(2)}) async-start(f32[64,8,256]{2,1,0:T(8,128)} %reshape_reshape.3), calls=%async_computation.1 | async-start | bytes 1048576 | tf_op jit(solution)/shard_map/all_to_all | solution.py:60
  173.5 0.6 fusion.40
  174.1 0.3 exponential_reduce_fusion
  174.4 0.3 fusion
  174.8 0.8 fusion.8
  175.5 0.3 fusion.6
  175.9 0.6 multiply_convert_fusion
  176.5 0.8 fusion.7
  177.3 1.0 fusion.9
  178.2 33.4 %all-to-all-done.1 = f32[64,8,256]{2,1,0:T(8,128)S(1)} async-done(((f32[64,8,256]{2,1,0:T(8,128)}), f32[64,8,256]{2,1,0:T(8,128)S(1)}, u32[]{:S(2)}, u32[]{:S(2)}) %all-to-all-start.1) | async-done | bytes 524320 | tf_op jit(solution)/shard_map/all_to_all | solution.py:60
  211.6 0.7 reduce_sum.87
  (18 shorter events, 0.2 us)
Async XLA Ops:
  7.2 105.6 %copy-start = (bf16[128,256]{1,0:T(8,128)(2,1)S(1)}, bf16[128,256]{1,0:T(8,128)(2,1)}, u32[]{:S(2)}) copy-start(bf16[128,256]{1,0:T(8,128)(2,1)} %param.13) | copy-start | bytes 196612
  12.7 20.2 %all-to-all-start = ((bf16[8,4,1,256]{3,1,2,0:T(4,128)(2,1)}), bf16[8,4,1,256]{3,1,2,0:T(4,128)(2,1)S(1)}, u32[]{:S(2)}, u32[]{:S(2)}) async-start(bf16[8,4,1,256]{3,1,2,0:T(4,128)(2,1)} %constant_dynamic-update-slice_fusion), calls=%async_computation | async-start | bytes 32768 | tf_op jit(solution)/shard_map/all_to_all | solution.py:145
  24.7 86.8 %all-gather.6.cloned.1.call-start = ((), (), s32[]{:S(2)}) async-start(), calls=%async_computation.2 | async-start | bytes 1976320 | tf_op jit(solution)/shard_map/all_gather | solution.py:111
  78.5 68.8 %copy-start.2 = (bf16[128,256]{1,0:T(8,128)(2,1)S(1)}, bf16[128,256]{1,0:T(8,128)(2,1)}, u32[]{:S(2)}) copy-start(bf16[128,256]{1,0:T(8,128)(2,1)} %param.14) | copy-start | bytes 196612
  111.5 35.8 %copy-start.1 = (bf16[512,1538]{0,1:T(8,128)(2,1)S(1)}, bf16[512,1538]{0,1:T(8,128)(2,1)}, u32[]{:S(2)}) copy-start(bf16[512,1538]{0,1:T(8,128)(2,1)} %all-gather.6.cloned.1.call-done) | copy-start | bytes 4724740
  151.5 60.1 %all-to-all-start.1 = ((f32[64,8,256]{2,1,0:T(8,128)}), f32[64,8,256]{2,1,0:T(8,128)S(1)}, u32[]{:S(2)}, u32[]{:S(2)}) async-start(f32[64,8,256]{2,1,0:T(8,128)} %reshape_reshape.3), calls=%async_computation.1 | async-start | bytes 1048576 | tf_op jit(solution)/shard_map/all_to_all | solution.py:60
Sparse Core Ops, SparseCore 0:
  78.6 32.8 all-gather.5
